TPU v7x, 32 devices: a whole 2x2x4 slice. The times are simulated.
32 devices in a mesh: img: 4 (over z), ref: 8 (over y, x, core).
Axes of the slice: x: 2, y: 2, z: 4, core: 2. Of those that a mesh axis runs over, the one named last changes fastest.
Arguments:
- images: bfloat16 [2048, 9216], P(('img', 'ref')), may hold values from -96 to 96
- references: bfloat16 [6912, 9216], P('ref'), may hold values from -0.5 to 0.5
- class_prior: float32 [192], P('ref'), may hold values from 0.2 to 5
Outputs:
- class_sums: float32 [192, 9216], P('ref', 'img')
- class_weights: float32 [192], P('ref')
All inputs are finite; a program needn't handle non-finite values.
Results may differ from a plain program's by a relative error of at most 0.0021.
Values may be sent and summed in bfloat16 or wider, within the bound.
No kernel may reach another device: no remote copies, remote signals or barrier semaphores. Data moves between devices by JAX's collectives and lax.ppermute only.
A program may use at most 128 MiB of HBM per device.

v0:
```python
import jax
import jax.numpy as jnp
from jax import lax
from jax.sharding import PartitionSpec as P

ANG = 144


def unturn(stacked, shift_size):
    classes_here, rotations, columns = stacked.shape
    cycles = stacked.reshape(classes_here, rotations, columns // ANG, ANG)
    doubled = jnp.concatenate([cycles, cycles], axis=3)
    result = doubled[:, 0, :, 0:ANG]
    for turn_index in range(1, rotations):
        start_col = turn_index * shift_size
        result = result + doubled[:, turn_index, :, start_col : start_col + ANG]
    return result.reshape(classes_here, columns)


def per_device(images, references, class_prior):
    local_refs, pixels = references.shape
    classes_here = class_prior.shape[0]
    rotations = local_refs // classes_here
    shift_size = ANG // rotations
    half_norm = 0.5 * jnp.einsum(
        "jp,jp->j", references, references, preferred_element_type=jnp.float32
    )
    offsets = (jnp.log(class_prior)[:, None] - half_norm.reshape(classes_here, rotations)).reshape(
        local_refs
    )
    gathered = lax.all_gather(images, "ref", axis=0, tiled=True)
    products = lax.dot_general(
        gathered, references, (((1,), (1,)), ((), ())), preferred_element_type=jnp.float32
    )
    scores = products + offsets
    local_max = jnp.max(scores, axis=1)
    top_score = lax.pmax(local_max, "ref")
    denominator = lax.psum(jnp.sum(jnp.exp(scores - top_score[:, None]), axis=1), "ref")
    weights = (jnp.exp(scores - top_score[:, None]) / denominator[:, None]).astype(jnp.bfloat16)
    local_mass = (
        jnp.sum(weights.astype(jnp.float32), axis=0).reshape(classes_here, rotations).sum(axis=1)
    )
    class_weights = lax.psum(local_mass, "img")
    sums = lax.dot_general(
        weights, gathered, (((0,), (0,)), ((), ())), preferred_element_type=jnp.float32
    )
    reduced = lax.psum_scatter(sums, "img", scatter_dimension=1, tiled=True)
    class_sums = unturn(reduced.reshape(classes_here, rotations, -1), shift_size)
    return (class_sums, class_weights)


def solution(mesh):
    placed = (P(("img", "ref"), None), P("ref", None), P("ref"))
    return jax.shard_map(
        per_device,
        mesh=mesh,
        in_specs=placed,
        out_specs=(P("ref", "img"), P("ref")),
        check_vma=False,
    )
```

profile of v0, /device:TPU:0, one launch (start us, length us, event | category | flops | bytes accessed | tf_op | source)
XLA Modules:
  0.0 719.0 jit_solution(10911316544609606139)
XLA Ops:
  7.2 0.0 all-gather.2.cloned.1.call-start
  7.2 0.7 all-gather.2.cloned.1.call-update
  7.9 0.0 reduce-scatter.2.cloned.1.call-start
  7.9 0.7 log.3
  8.6 0.1 sub.24
  8.7 0.1 sub.25
  8.8 7.0 fusion
  15.8 55.7 %all-gather.2.cloned.1.call-done = bf16[512,9216]{1,0:T(8,128)(2,1)} async-done(((bf16[64,9216]{1,0:T(8,128)(2,1)}), bf16[512,9216]{1,0:T(8,128)(2,1)}) %all-gather.2.cloned.1.call-update) | async-done | bytes 9437200 | tf_op jit(solution)/shard_map/all_gather | solution.py:31
  71.4 14.2 %add_reduce_fusion = (f32[512]{0:T(512)S(1)}, f32[512,864]{0,1:T(8,128)S(1)}) fusion(f32[864]{0:T(1024)S(1)} %multiply_subtract_fusion, bf16[512,9216]{1,0:T(8,128)(2,1)} %all-gather.2.cloned.1.call-done, bf16[864,9216]{1,0:T(8,128)(2,1)} %param.4), kind=kOutput, calls=%fused_computation.5 | convolution fusion | flops 8154611200 | bytes 27137408 | tf_op jit(solution)/shard_map/dot_general | solution.py:32
  85.6 13.1 %pmax.7 = f32[512]{0:T(512)S(1)} all-reduce(f32[512]{0:T(512)S(1)} %get-tuple-element.22), channel_id=1, replica_groups=mesh['img'=4,'ref'=8] {'ref'}, use_global_device_ids=true, to_apply=%region_1.0 | all-reduce | flops 512 | bytes 4096 | tf_op jit(solution)/shard_map/pmax | solution.py:37
  98.7 0.4 fusion.1
  99.1 11.8 %psum.14 = f32[512]{0:T(512)S(1)} all-reduce(f32[512]{0:T(512)S(1)} %fusion.1), channel_id=1, replica_groups=mesh['img'=4,'ref'=8] {'ref'}, use_global_device_ids=true, to_apply=%region_3.0 | all-reduce | flops 512 | bytes 4096 | tf_op jit(solution)/shard_map/psum | solution.py:38
  110.9 0.5 convert_reduce_fusion
  111.4 17.6 %fusion.2 = f32[864,9216]{1,0:T(8,128)} fusion(bf16[512,864]{0,1:T(8,128)(2,1)S(1)} %get-tuple-element.3, bf16[512,9216]{1,0:T(8,128)(2,1)} %all-gather.2.cloned.1.call-done), kind=kOutput, calls=%fused_computation.44 | convolution fusion | flops 8153726976 | bytes 42172416 | tf_op jit(solution)/shard_map/dot_general | solution.py:44
  129.0 0.0 reduce-scatter.2.cloned.1.call-update
  129.0 0.1 reshape.59
  129.1 0.1 reduce_sum.29
  129.2 12.4 %psum.15 = f32[24]{0:T(128)} all-reduce(f32[24]{0:T(128)S(1)} %reduce_sum.29), channel_id=1, replica_groups=mesh['img'=4,'ref'=8] {'img'}, use_global_device_ids=true, to_apply=%region_7.0 | all-reduce | flops 24 | bytes 192 | tf_op jit(solution)/shard_map/psum | solution.py:43
  141.6 513.8 %reduce-scatter.2.cloned.1.call-done = f32[864,2304]{1,0:T(8,128)} async-done(((f32[864,9216]{1,0:T(8,128)}), f32[864,2304]{1,0:T(8,128)}) %reduce-scatter.2.cloned.1.call-update) | async-done | bytes 7962640 | tf_op jit(solution)/shard_map/reduce_scatter | solution.py:47
  655.4 15.2 %reshape_reshape.3 = f32[24,36,16,144]{3,2,1,0:T(8,128)} reshape(f32[864,2304]{1,0:T(8,128)} %reduce-scatter.2.cloned.1.call-done) | data formatting | bytes 15925248 | tf_op jit(solution)/shard_map/reshape;reshape | solution.py:11
  670.6 0.0 copy-start
  670.6 8.5 %maximum_add_fusion = f32[24,1,16,144]{3,2,1,0:T(8,128)} fusion(f32[24,36,16,144]{3,2,1,0:T(8,128)} %reshape_reshape.3), kind=kLoop, calls=%fused_computation.26 | loop fusion | flops 1769472 | bytes 14770176 | tf_op jit(solution)/shard_map/add | solution.py:16
  679.1 0.2 copy-done
  679.3 1.0 pad_maximum_fusion
  680.2 3.5 pad_maximum_fusion.18
  683.7 2.5 pad_maximum_fusion.17
  686.2 1.9 reshape.71
  688.1 1.9 squeeze.128
  690.0 1.9 squeeze.111
  691.9 1.9 squeeze.110
  693.8 1.9 squeeze.126
  695.6 1.9 squeeze.118
  697.5 1.9 squeeze.122
  699.4 1.9 squeeze.117
  701.3 1.9 squeeze.124
  703.2 1.9 squeeze.116
  705.1 1.9 squeeze.121
  707.0 0.9 squeeze.115
  707.8 0.2 squeeze.125
  708.0 0.2 squeeze.114
  708.3 0.2 squeeze.120
  708.5 0.2 squeeze.113
  708.7 0.2 squeeze.123
  708.9 0.2 squeeze.112
  709.1 0.2 squeeze.119
  709.3 0.2 squeeze.127
  709.5 2.7 add_add_fusion
  (1 shorter events, 0.0 us)
Async XLA Ops:
  7.2 64.3 %all-gather.2.cloned.1.call-start = ((), (), s32[]{:S(2)}) async-start(), calls=%async_computation.1 | async-start | bytes 10616832 | tf_op jit(solution)/shard_map/all_gather | solution.py:31
  7.9 647.5 %reduce-scatter.2.cloned.1.call-start = ((), (), s32[]{:S(2)}) async-start(), calls=%async_computation.2 | async-start | bytes 39813120 | tf_op jit(solution)/shard_map/reduce_scatter | solution.py:47
  670.6 8.6 %copy-start = (f32[24,36,16,144]{3,2,1,0:T(8,128)S(1)}, f32[24,36,16,144]{3,2,1,0:T(8,128)}, u32[]{:S(2)}) copy-start(f32[24,36,16,144]{3,2,1,0:T(8,128)} %reshape_reshape.3) | copy-start | bytes 23887876
Sparse Core Ops, SparseCore 0:
  9.9 61.5 all-gather.1
  129.1 526.1 reduce-scatter.1
where the time goes:
time: 720 us; the launch traced here: 719 us
  waiting for transfers between devices  570 us (79%)
  local copies, waits for them, and re-layouts  39.7 us (6%)
  blocking collectives  37.3 us (5%)
  matrix products  31.7 us (4%)
  other arithmetic  26.1 us (4%)
  between operations  14.1 us (2%)
    reduce_scatter x1, waiting for transfers between devices, per_device(): reduced = lax.psum_scatter(sums, 'img', scatter_dimension=1, tiled=True)  514 us
    all_gather x1, waiting for transfers between devices, per_device(): gathered = lax.all_gather(images, 'ref', axis=0, tiled=True)  55.7 us
    squeeze x19, local copies, waits for them, and re-layouts, unturn(): result = result + doubled[:, turn_index, :, start_col:start_col + ANG]  21.4 us
    dot_general x1, matrix products, per_device(): lax.dot_general(weights, gathered, (((0,), (0,)), ((), ())), preferred_el...  17.6 us
    another operation x1, local copies, waits for them, and re-layouts, unturn(): cycles = stacked.reshape(classes_here, rotations, columns // ANG, ANG)  15.2 us
  transfers between devices with their start and end apart: 2, of which 2 were waited for; matrix products, arithmetic and copies ran while one was open for 1% of the time, Pallas kernels for 0%

commit v1 on v0

--- a/solution.py
+++ b/solution.py
@@ -1,9 +1,46 @@
+import functools
 import jax
 import jax.numpy as jnp
 from jax import lax
 from jax.sharding import PartitionSpec as P
+from jax.lax import axis_index, axis_size, ppermute
 
 ANG = 144
+
+
+def follow_pipes_here(v0, axis_no):
+    v0 = jnp.moveaxis(v0, 0, axis_no)
+    out_arr = v0.shape
+    return v0.reshape(
+        *out_arr[:axis_no], out_arr[axis_no] * out_arr[axis_no + 1], *out_arr[axis_no + 2 :]
+    )
+
+
+def save_the_region(content, across, k_dim):
+    count_all = axis_size(across)
+    q_next = map(lambda tick: (tick, (tick + 1) % count_all), range(count_all))
+    chunks = list(q_next)
+    frames = [(b, pp) for pp, b in chunks]
+    oldest, current_value = ([], [])
+    for dev_j in range(count_all - 1):
+        if dev_j % 2 == 0:
+            arr_next = ppermute(oldest[-1] if oldest else content, axis_name=across, perm=chunks)
+            oldest.append(arr_next)
+        else:
+            current_value.append(
+                ppermute(
+                    current_value[-1] if current_value else content, axis_name=across, perm=frames
+                )
+            )
+    f_now = jnp.stack([*oldest[::-1], content, *current_value], 0)
+    r2 = axis_index(across)
+    m_next = len(oldest)
+    a_next = r2 - m_next
+    f_now = f_now[(jnp.arange(count_all) - a_next) % count_all]
+    return follow_pipes_here(f_now, k_dim)
+
+
+shelves_watch = functools.partial(save_the_region, across="ref", k_dim=0)
 
 
 def unturn(stacked, shift_size):
@@ -28,7 +65,7 @@
     offsets = (jnp.log(class_prior)[:, None] - half_norm.reshape(classes_here, rotations)).reshape(
         local_refs
     )
-    gathered = lax.all_gather(images, "ref", axis=0, tiled=True)
+    gathered = shelves_watch(images)
     products = lax.dot_general(
         gathered, references, (((1,), (1,)), ((), ())), preferred_element_type=jnp.float32
     )

time: 720 us -> 775 us (1.076)
  waiting for transfers between devices: 570 us -> 596 us
  local copies, waits for them, and re-layouts: 39.7 us -> 58.6 us
  starting transfers between devices: 0.08 us -> 8.58 us
    ppermute x0 -> x7, waiting for transfers between devices: none -> 81.3 us  [the longest x4 81.3 us: save_the_region(): ppermute(oldest[-1] if oldest else content, axis_name=across, perm=chunks)]
    all_gather x1 -> x0, waiting for transfers between devices: 55.7 us -> none  [per_device(): gathered = lax.all_gather(images, 'ref', axis=0, tiled=True)]
    unnamed x2 -> x11, local copies, waits for them, and re-layouts: 0.17 us -> 9.14 us
    gather x0 -> x1, local copies, waits for them, and re-layouts: none -> 8.78 us  [save_the_region(): f_now = f_now[(jnp.arange(count_all) - a_next) % count_all]]
    ppermute x0 -> x7, starting transfers between devices: none -> 8.54 us  [the longest x3 8.03 us: save_the_region(): ppermute(current_value[-1] if current_value else content, axis_name=acros...]
  transfers between devices with their start and end apart: 2 -> 8, of which waited for: 2 -> 5; matrix products, arithmetic and copies ran while one was open for 1% -> 2% of each run, Pallas kernels for 0% -> 0%
where the time goes in v1:
time: 775 us; the launch traced here: 774 us
  waiting for transfers between devices  596 us (77%)
  local copies, waits for them, and re-layouts  58.6 us (8%)
  blocking collectives  38.7 us (5%)
  matrix products  31.7 us (4%)
  other arithmetic  26.1 us (3%)
  between operations  14.1 us (2%)
  starting transfers between devices  8.58 us (1%)
    reduce_scatter x1, waiting for transfers between devices, per_device(): reduced = lax.psum_scatter(sums, 'img', scatter_dimension=1, tiled=True)  515 us
    ppermute x4, waiting for transfers between devices, save_the_region(): ppermute(oldest[-1] if oldest else content, axis_name=across, perm=chunks)  81.3 us
    squeeze x19, local copies, waits for them, and re-layouts, unturn(): result = result + doubled[:, turn_index, :, start_col:start_col + ANG]  21.4 us
    dot_general x1, matrix products, per_device(): lax.dot_general(weights, gathered, (((0,), (0,)), ((), ())), preferred_el...  17.6 us
  transfers between devices with their start and end apart: 8, of which 5 were waited for; matrix products, arithmetic and copies ran while one was open for 2% of the time, Pallas kernels for 0%

profile of v1, /device:TPU:0, one launch (start us, length us, event | category | flops | bytes accessed | tf_op | source)
XLA Modules:
  0.0 773.9 jit_solution(7398608951243656478)
XLA Ops:
  7.2 0.5 collective-permute-start
  7.7 17.0 %collective-permute-done = bf16[64,9216]{1,0:T(8,128)(2,1)S(1)} collective-permute-done((bf16[64,9216]{1,0:T(8,128)(2,1)}, bf16[64,9216]{1,0:T(8,128)(2,1)S(1)}, u32[]{:S(2)}, u32[]{:S(2)}) %collective-permute-start) | collective-permute-done | bytes 1179680 | tf_op jit(solution)/shard_map/ppermute | solution.py:27
  24.7 2.6 collective-permute-start.4
  27.3 24.5 %collective-permute-done.1 = bf16[64,9216]{1,0:T(8,128)(2,1)S(1)} collective-permute-done((bf16[64,9216]{1,0:T(8,128)(2,1)S(1)}, bf16[64,9216]{1,0:T(8,128)(2,1)S(1)}, u32[]{:S(2)}, u32[]{:S(2)}) %collective-permute-start.1) | collective-permute-done | bytes 1179680 | tf_op jit(solution)/shard_map/ppermute | solution.py:27
  51.9 0.7 log.3
  52.8 2.7 collective-permute-start.5
  55.5 24.3 %collective-permute-done.2 = bf16[64,9216]{1,0:T(8,128)(2,1)} collective-permute-done((bf16[64,9216]{1,0:T(8,128)(2,1)S(1)}, bf16[64,9216]{1,0:T(8,128)(2,1)}, u32[]{:S(2)}, u32[]{:S(2)}) %collective-permute-start.2) | collective-permute-done | bytes 1179680 | tf_op jit(solution)/shard_map/ppermute | solution.py:27
  79.7 7.0 fusion
  86.8 2.7 collective-permute-start.6
  89.4 15.5 %collective-permute-done.3 = bf16[64,9216]{1,0:T(8,128)(2,1)S(1)} collective-permute-done((bf16[64,9216]{1,0:T(8,128)(2,1)}, bf16[64,9216]{1,0:T(8,128)(2,1)S(1)}, u32[]{:S(2)}, u32[]{:S(2)}) %collective-permute-start.3) | collective-permute-done | bytes 1179680 | tf_op jit(solution)/shard_map/ppermute | solution.py:27
  105.0 1.1 bitcast_dynamic-update-slice_fusion.7
  106.1 2.4 bitcast_dynamic-update-slice_fusion.6
  108.5 1.1 bitcast_dynamic-update-slice_fusion.5
  109.6 1.1 bitcast_dynamic-update-slice_fusion.4
  110.6 1.1 bitcast_dynamic-update-slice_fusion.3
  111.8 1.1 bitcast_dynamic-update-slice_fusion.2
  112.9 1.1 bitcast_dynamic-update-slice_fusion.1
  114.0 1.2 bitcast_dynamic-update-slice_fusion
  115.2 8.8 %gather_fusion = bf16[8,64,9216]{2,1,0:T(8,128)(2,1)} fusion(bf16[8,64,9216]{2,1,0:T(8,128)(2,1)} %bitcast_dynamic-update-slice_fusion, s32[1024]{0:T(1024)S(1)} %pad_clamp_fusion), kind=kCustom, calls=%fused_computation | custom fusion | bytes 18874400 | tf_op jit(solution)/shard_map/gather | solution.py:39
  123.9 14.2 %add_reduce_fusion = (f32[512]{0:T(512)S(1)}, f32[512,864]{0,1:T(8,128)S(1)}) fusion(f32[864]{0:T(1024)S(1)} %multiply_subtract_fusion, bf16[512,9216]{1,0:T(8,128)(2,1)} %bitcast.63, bf16[864,9216]{1,0:T(8,128)(2,1)} %param.4), kind=kOutput, calls=%fused_computation.6 | convolution fusion | flops 8154611200 | bytes 27137408 | tf_op jit(solution)/shard_map/dot_general | solution.py:69
  138.1 11.9 %pmax.7 = f32[512]{0:T(512)S(1)} all-reduce(f32[512]{0:T(512)S(1)} %get-tuple-element.22), channel_id=1, replica_groups=mesh['img'=4,'ref'=8] {'ref'}, use_global_device_ids=true, to_apply=%region_1.2 | all-reduce | flops 512 | bytes 4096 | tf_op jit(solution)/shard_map/pmax | solution.py:74
  150.0 0.4 fusion.1
  150.3 14.3 %psum.14 = f32[512]{0:T(512)S(1)} all-reduce(f32[512]{0:T(512)S(1)} %fusion.1), channel_id=1, replica_groups=mesh['img'=4,'ref'=8] {'ref'}, use_global_device_ids=true, to_apply=%region_3.4 | all-reduce | flops 512 | bytes 4096 | tf_op jit(solution)/shard_map/psum | solution.py:75
  164.6 0.5 convert_reduce_fusion
  165.2 17.6 %fusion.4 = f32[864,9216]{1,0:T(8,128)} fusion(bf16[512,864]{0,1:T(8,128)(2,1)S(1)} %get-tuple-element.3, bf16[512,9216]{1,0:T(8,128)(2,1)} %bitcast.64), kind=kOutput, calls=%fused_computation.60 | convolution fusion | flops 8153726976 | bytes 42172416 | tf_op jit(solution)/shard_map/dot_general | solution.py:81
  183.0 12.6 %psum.15 = f32[24]{0:T(128)} all-reduce(f32[24]{0:T(128)S(1)} %reduce_sum.29), channel_id=1, replica_groups=mesh['img'=4,'ref'=8] {'img'}, use_global_device_ids=true, to_apply=%region_7.8 | all-reduce | flops 24 | bytes 192 | tf_op jit(solution)/shard_map/psum | solution.py:80
  195.6 514.6 %reduce-scatter.2.cloned.1.call-done = f32[864,2304]{1,0:T(8,128)} async-done(((f32[864,9216]{1,0:T(8,128)}), f32[864,2304]{1,0:T(8,128)}) %reduce-scatter.2.cloned.1.call-update) | async-done | bytes 7962640 | tf_op jit(solution)/shard_map/reduce_scatter | solution.py:84
  710.2 15.2 %reshape_reshape.3 = f32[24,36,16,144]{3,2,1,0:T(8,128)} reshape(f32[864,2304]{1,0:T(8,128)} %reduce-scatter.2.cloned.1.call-done) | data formatting | bytes 15925248 | tf_op jit(solution)/shard_map/reshape;reshape | solution.py:48
  725.4 8.5 %maximum_add_fusion = f32[24,1,16,144]{3,2,1,0:T(8,128)} fusion(f32[24,36,16,144]{3,2,1,0:T(8,128)} %reshape_reshape.3), kind=kLoop, calls=%fused_computation.35 | loop fusion | flops 1769472 | bytes 14770176 | tf_op jit(solution)/shard_map/add | solution.py:53
  734.1 1.0 pad_maximum_fusion
  735.0 3.5 pad_maximum_fusion.18
  738.5 2.5 pad_maximum_fusion.17
  741.0 1.9 reshape.132
  742.9 1.9 squeeze.128
  744.8 1.9 squeeze.111
  746.7 1.9 squeeze.110
  748.6 1.9 squeeze.126
  750.4 1.9 squeeze.118
  752.3 1.9 squeeze.122
  754.2 1.9 squeeze.117
  756.1 1.9 squeeze.124
  758.0 1.9 squeeze.116
  759.9 1.9 squeeze.121
  761.8 0.9 squeeze.115
  763.1 0.2 squeeze.120
  763.3 0.2 squeeze.113
  763.9 0.2 squeeze.119
  764.3 2.7 add_add_fusion
  (24 shorter events, 1.7 us)
Async XLA Ops:
  7.2 703.0 %reduce-scatter.2.cloned.1.call-start = ((), (), s32[]{:S(2)}) async-start(), calls=%async_computation.1 | async-start | bytes 39813120 | tf_op jit(solution)/shard_map/reduce_scatter | solution.py:84
  7.2 17.5 %collective-permute-start = (bf16[64,9216]{1,0:T(8,128)(2,1)}, bf16[64,9216]{1,0:T(8,128)(2,1)S(1)}, u32[]{:S(2)}, u32[]{:S(2)}) collective-permute-start(bf16[64,9216]{1,0:T(8,128)(2,1)} %param.3), channel_id=1, source_target_pairs={{0,1},{1,2},{2,3},{3,4},{4,5},{5,6},{6,7},{7,0},{8,9},{9,10},{10,1... | collective-permute-start | bytes 3538952 | tf_op jit(solution)/shard_map/ppermute | solution.py:27
  24.7 27.2 %collective-permute-start.1 = (bf16[64,9216]{1,0:T(8,128)(2,1)S(1)}, bf16[64,9216]{1,0:T(8,128)(2,1)S(1)}, u32[]{:S(2)}, u32[]{:S(2)}) collective-permute-start(bf16[64,9216]{1,0:T(8,128)(2,1)S(1)} %collective-permute-done), channel_id=1, source_target_pairs={{0,1},{1,2},{2,3},{3,4},{4,5},{5,6},{6,7},{7,0},{8,9},{9,10},{10,1... | collective-permute-start | bytes 3538952 | tf_op jit(solution)/shard_map/ppermute | solution.py:27
  24.7 28.1 %collective-permute-start.4 = (bf16[64,9216]{1,0:T(8,128)(2,1)}, bf16[64,9216]{1,0:T(8,128)(2,1)S(1)}, u32[]{:S(2)}, u32[]{:S(2)}) collective-permute-start(bf16[64,9216]{1,0:T(8,128)(2,1)} %param.3), channel_id=1, source_target_pairs={{1,0},{2,1},{3,2},{4,3},{5,4},{6,5},{7,6},{0,7},{9,8},{10,9},{11,1... | collective-permute-start | bytes 3538952 | tf_op jit(solution)/shard_map/ppermute | solution.py:31
  51.9 27.9 %collective-permute-start.2 = (bf16[64,9216]{1,0:T(8,128)(2,1)S(1)}, bf16[64,9216]{1,0:T(8,128)(2,1)}, u32[]{:S(2)}, u32[]{:S(2)}) collective-permute-start(bf16[64,9216]{1,0:T(8,128)(2,1)S(1)} %collective-permute-done.1), channel_id=1, source_target_pairs={{0,1},{1,2},{2,3},{3,4},{4,5},{5,6},{6,7},{7,0},{8,9},{9,10},{10,1... | collective-permute-start | bytes 3538952 | tf_op jit(solution)/shard_map/ppermute | solution.py:27
  52.8 57.9 %copy-start.1 = (bf16[64,9216]{1,0:T(8,128)(2,1)S(1)}, bf16[64,9216]{1,0:T(8,128)(2,1)}, u32[]{:S(2)}) copy-start(bf16[64,9216]{1,0:T(8,128)(2,1)} %param.3) | copy-start | bytes 3538948
  52.8 34.0 %collective-permute-start.5 = (bf16[64,9216]{1,0:T(8,128)(2,1)S(1)}, bf16[64,9216]{1,0:T(8,128)(2,1)S(1)}, u32[]{:S(2)}, u32[]{:S(2)}) collective-permute-start(bf16[64,9216]{1,0:T(8,128)(2,1)S(1)} %collective-permute-done.4), channel_id=1, source_target_pairs={{1,0},{2,1},{3,2},{4,3},{5,4},{6,5},{7,6},{0,7},{9,8},{10,9},{11,1... | collective-permute-start | bytes 3538952 | tf_op jit(solution)/shard_map/ppermute | solution.py:31
  79.7 25.2 %collective-permute-start.3 = (bf16[64,9216]{1,0:T(8,128)(2,1)}, bf16[64,9216]{1,0:T(8,128)(2,1)S(1)}, u32[]{:S(2)}, u32[]{:S(2)}) collective-permute-start(bf16[64,9216]{1,0:T(8,128)(2,1)} %collective-permute-done.2), channel_id=1, source_target_pairs={{0,1},{1,2},{2,3},{3,4},{4,5},{5,6},{6,7},{7,0},{8,9},{9,10},{10,1... | collective-permute-start | bytes 3538952 | tf_op jit(solution)/shard_map/ppermute | solution.py:27
  86.8 27.2 %collective-permute-start.6 = (bf16[64,9216]{1,0:T(8,128)(2,1)S(1)}, bf16[64,9216]{1,0:T(8,128)(2,1)S(1)}, u32[]{:S(2)}, u32[]{:S(2)}) collective-permute-start(bf16[64,9216]{1,0:T(8,128)(2,1)S(1)} %collective-permute-done.5), channel_id=1, source_target_pairs={{1,0},{2,1},{3,2},{4,3},{5,4},{6,5},{7,6},{0,7},{9,8},{10,9},{11,1... | collective-permute-start | bytes 3538952 | tf_op jit(solution)/shard_map/ppermute | solution.py:31
  725.4 8.6 %copy-start = (f32[24,36,16,144]{3,2,1,0:T(8,128)S(1)}, f32[24,36,16,144]{3,2,1,0:T(8,128)}, u32[]{:S(2)}) copy-start(f32[24,36,16,144]{3,2,1,0:T(8,128)} %reshape_reshape.3) | copy-start | bytes 23887876
Sparse Core Ops, SparseCore 0:
  182.9 527.2 reduce-scatter.1
